TPU v7x, 128 devices: a whole 4x4x4 slice. The times are simulated.
128 devices in a mesh: node: 8 (over z, core), local: 16 (over x, y).
Axes of the slice: x: 4, y: 4, z: 4, core: 2. Of those that a mesh axis runs over, the one named last changes fastest.
Arguments:
- tokens: bfloat16 [16384, 4096], P(('node', 'local')), may hold values from -6 to 6
- cotangent: bfloat16 [16384, 4096], P(('node', 'local')), may hold values from -6 to 6
- gate_probs: float32 [16384, 8], P(('node', 'local')), may hold values from 0.02 to 0.5
- experts: int32 [16384, 8], P(('node', 'local')), may hold values from 0 to 127, all different within a row; in each aligned block of 128 rows (0 to 127, 128 to 255, ...) at most 10 rows name the same one
- stratum: int32 [128], P(('node', 'local')), may hold values from 0 to 7
- token_level: int32 [16384], P(('node', 'local')), may hold values from 0 to 63
- w_gate_up: bfloat16 [128, 4096, 1024], P(('node', 'local')), may hold values from -0.09375 to 0.09375
- w_down: bfloat16 [128, 512, 4096], P(('node', 'local')), may hold values from -0.25 to 0.25
Outputs:
- grad_tokens: bfloat16 [16384, 4096], P(('node', 'local'))
- grad_probs: bfloat16 [16384, 8], P(('node', 'local'))
Inputs may be any that keep to these rules, and one draw needn't show every extreme that they name: Among the tokens of one device no expert is named more than 10 times; in every draw some expert is named exactly 10 times by the tokens of some device. A token names 8 different experts.
All inputs are finite; a program needn't handle non-finite values.
Results may differ from a plain program's by a relative error of at most 0.013.
Values may be sent and summed in bfloat16 or wider, within the bound.
No kernel may reach another device: no remote copies, remote signals or barrier semaphores. Data moves between devices by JAX's collectives and lax.ppermute only.
A program may use at most 192 MiB of HBM per device.

v0:
```python
import jax
import jax.numpy as jnp
from jax import lax
from jax.sharding import PartitionSpec as P

STRATA = 8
LEVELS = 64


def expert_grads(inputs, upstream, weight_in, weight_out):
    hidden_units = weight_out.shape[0]
    projected = jnp.dot(inputs, weight_in, preferred_element_type=jnp.float32)
    gate_part = projected[:, :hidden_units]
    up_part = projected[:, hidden_units:]
    sigmoid_gate = jax.nn.sigmoid(gate_part)
    activated = gate_part * sigmoid_gate
    hidden = (activated * up_part).astype(jnp.bfloat16)
    backward = jnp.dot(upstream, weight_out.T, preferred_element_type=jnp.float32)
    prob_grad = jnp.sum(hidden.astype(jnp.float32) * backward, axis=1).astype(jnp.bfloat16)
    grad_gate = backward * up_part * sigmoid_gate * (1.0 + gate_part * (1.0 - sigmoid_gate))
    grad_up = backward * activated
    stacked = jnp.concatenate([grad_gate, grad_up], axis=1).astype(jnp.bfloat16)
    row_grads = jnp.dot(stacked, weight_in.T, preferred_element_type=jnp.float32).astype(
        jnp.bfloat16
    )
    return (row_grads, prob_grad)


def body(tokens, cotangent, gate_probs, experts, stratum, token_level, w_gate_up, w_down):
    device_count = lax.axis_size(("node", "local"))
    token_rows, chosen_count = experts.shape
    width = tokens.shape[1]
    capacity = max(2, token_rows * chosen_count * 5 // (4 * device_count))
    stratum_here = stratum[0]
    masked = token_level * STRATA < (stratum_here + 1) * LEVELS
    loss_weight = jnp.where(
        masked, STRATA / (stratum_here + 1).astype(jnp.float32), jnp.float32(0.0)
    )
    upstream = (cotangent.astype(jnp.float32) * loss_weight[:, None]).astype(jnp.bfloat16)
    chosen = experts.reshape(-1)
    pair_count = chosen.shape[0]
    onehot = (chosen[:, None] == jnp.arange(device_count, dtype=jnp.int32)[None, :]).astype(
        jnp.int32
    )
    ranking = jnp.sum((jnp.cumsum(onehot, axis=0) - 1) * onehot, axis=1)
    placed = chosen * capacity + ranking
    owner_table = jnp.full((device_count * capacity,), pair_count, jnp.int32)
    owner_table = owner_table.at[placed].set(jnp.arange(pair_count, dtype=jnp.int32))
    token_index = owner_table // chosen_count
    padded_tokens = jnp.concatenate([tokens, jnp.zeros((1, width), jnp.bfloat16)], axis=0)
    padded_upstream = jnp.concatenate([upstream, jnp.zeros((1, width), jnp.bfloat16)], axis=0)
    send_tokens = padded_tokens[token_index].reshape(device_count, capacity, width)
    send_upstream = padded_upstream[token_index].reshape(device_count, capacity, width)
    weight_in = w_gate_up[0]
    weight_out = w_down[0]
    arrived_tokens = lax.all_to_all(
        send_tokens, ("node", "local"), split_axis=0, concat_axis=0, tiled=True
    )
    sources = arrived_tokens.shape[0]
    items = arrived_tokens.shape[1]
    row_grads, prob_grad = expert_grads(
        arrived_tokens.reshape(sources * items, width),
        lax.all_to_all(
            send_upstream, ("node", "local"), split_axis=0, concat_axis=0, tiled=True
        ).reshape(sources * items, width),
        weight_in,
        weight_out,
    )
    row_grads, prob_grad = (
        row_grads.reshape(sources, items, width),
        prob_grad.reshape(sources, items),
    )
    home_grads = lax.all_to_all(
        row_grads, ("node", "local"), split_axis=0, concat_axis=0, tiled=True
    )
    home_probs = lax.all_to_all(
        prob_grad, ("node", "local"), split_axis=0, concat_axis=0, tiled=True
    )
    pair_grads = home_grads.reshape(device_count * capacity, width)[placed]
    weighted = (
        pair_grads.astype(jnp.float32).reshape(token_rows, chosen_count, width)
        * gate_probs[:, :, None]
    )
    grad_tokens = jnp.sum(weighted, axis=1).astype(jnp.bfloat16)
    grad_probs = home_probs.reshape(-1)[placed].reshape(token_rows, chosen_count)
    return (grad_tokens, grad_probs)


def solution(mesh):
    placed = (
        P(("node", "local"), None),
        P(("node", "local"), None),
        P(("node", "local"), None),
        P(("node", "local"), None),
        P(("node", "local")),
        P(("node", "local")),
        P(("node", "local"), None, None),
        P(("node", "local"), None, None),
    )
    return jax.shard_map(
        body,
        mesh=mesh,
        in_specs=placed,
        out_specs=(P(("node", "local"), None), P(("node", "local"), None)),
        check_vma=False,
    )
```

profile of v0, /device:TPU:1, one launch (start us, length us, event | category | flops | bytes accessed | tf_op | source)
XLA Modules:
  0.0 906.0 jit_solution(16173364798717366131)
XLA Ops:
  4.0 4.3 scatter_custom_fusion
  8.3 1.3 concatenate.11
  9.7 8.4 gather_fusion.1
  18.0 15.2 %reshape.108 = bf16[128,10,4096]{2,1,0:T(8,128)(2,1)} reshape(bf16[1280,4096]{1,0:T(8,128)(2,1)} %gather_fusion.1) | data formatting | bytes 20971520 | tf_op jit(solution)/shard_map/reshape | solution.py:52
  33.2 11.9 %all-to-all-start.1 = ((bf16[128,10,4096]{2,1,0:T(8,128)(2,1)}), bf16[128,10,4096]{2,1,0:T(8,128)(2,1)}, u32[]{:S(2)}, u32[]{:S(2)}) async-start(bf16[128,10,4096]{2,1,0:T(8,128)(2,1)} %reshape.108), calls=%async_computation.1 | async-start | bytes 33554432 | tf_op jit(solution)/shard_map/all_to_all | solution.py:56
  46.3 8.3 gather_fusion
  54.5 15.2 %reshape.106 = bf16[128,10,4096]{2,1,0:T(8,128)(2,1)} reshape(bf16[1280,4096]{1,0:T(8,128)(2,1)} %gather_fusion) | data formatting | bytes 20971520 | tf_op jit(solution)/shard_map/reshape | solution.py:53
  69.7 212.6 %all-to-all-done.1 = bf16[128,10,4096]{2,1,0:T(8,128)(2,1)} async-done(((bf16[128,10,4096]{2,1,0:T(8,128)(2,1)}), bf16[128,10,4096]{2,1,0:T(8,128)(2,1)}, u32[]{:S(2)}, u32[]{:S(2)}) %all-to-all-start.1) | async-done | bytes 10485792 | tf_op jit(solution)/shard_map/all_to_all | solution.py:56
  282.3 14.2 %all-to-all-start = ((bf16[128,10,4096]{2,1,0:T(8,128)(2,1)}), bf16[128,10,4096]{2,1,0:T(8,128)(2,1)}, u32[]{:S(2)}, u32[]{:S(2)}) async-start(bf16[128,10,4096]{2,1,0:T(8,128)(2,1)} %reshape.106), calls=%async_computation | async-start | bytes 33554432 | tf_op jit(solution)/shard_map/all_to_all | solution.py:63
  296.5 16.6 %reshape.109 = bf16[1280,4096]{1,0:T(8,128)(2,1)} reshape(bf16[128,10,4096]{2,1,0:T(8,128)(2,1)} %all-to-all-done.1) | data formatting | bytes 20971520 | tf_op jit(solution)/shard_map/reshape | solution.py:62
  313.1 17.5 %fusion.2 = f32[1280,1024]{0,1:T(8,128)} fusion(bf16[1280,4096]{1,0:T(8,128)(2,1)} %reshape.109, bf16[1,4096,1024]{2,1,0:T(8,128)(2,1)} %param.14), kind=kOutput, calls=%fused_computation.9 | convolution fusion | flops 10737418240 | bytes 24117248 | tf_op jit(solution)/shard_map/dot_general | solution.py:12
  330.5 204.3 %all-to-all-done = bf16[128,10,4096]{2,1,0:T(8,128)(2,1)} async-done(((bf16[128,10,4096]{2,1,0:T(8,128)(2,1)}), bf16[128,10,4096]{2,1,0:T(8,128)(2,1)}, u32[]{:S(2)}, u32[]{:S(2)}) %all-to-all-start) | async-done | bytes 10485792 | tf_op jit(solution)/shard_map/all_to_all | solution.py:63
  534.9 16.5 %reshape.107 = bf16[1280,4096]{1,0:T(8,128)(2,1)} reshape(bf16[128,10,4096]{2,1,0:T(8,128)(2,1)} %all-to-all-done) | data formatting | bytes 20971520 | tf_op jit(solution)/shard_map/reshape | solution.py:65
  551.4 12.7 %multiply_reduce_fusion = (bf16[1280]{0:T(1024)(128)(2,1)S(1)}, bf16[1280,512]{0,1:T(8,128)(2,1)S(1)}, bf16[1280,512]{0,1:T(8,128)(2,1)S(1)}) fusion(f32[1280,1024]{0,1:T(8,128)} %fusion.2, bf16[1280,4096]{1,0:T(8,128)(2,1)} %reshape.107, bf16[1,512,4096]{2,1,0:T(8,128)(2,1)} %param.15), kind=kOutput, calls=%fused_computation.16 | convolution fusion | flops 5380504576 | bytes 22546944 | tf_op jit(solution)/shard_map/dot_general | solution.py:18
  564.1 0.8 convert_element_type.62
  564.9 11.7 %all-to-all-start.3 = ((bf16[128,1,10]{2,1,0:T(2,128)(2,1)}), bf16[128,1,10]{2,1,0:T(2,128)(2,1)S(1)}, u32[]{:S(2)}, u32[]{:S(2)}) async-start(bf16[128,1,10]{2,1,0:T(2,128)(2,1)} %convert_element_type.62), calls=%async_computation.3 | async-start | bytes 131072 | tf_op jit(solution)/shard_map/all_to_all | solution.py:76
  576.5 17.1 %convolution_convert_fusion = bf16[1280,4096]{1,0:T(8,128)(2,1)} fusion(bf16[1,4096,1024]{2,1,0:T(8,128)(2,1)} %param.14, bf16[1280,512]{0,1:T(8,128)(2,1)S(1)} %get-tuple-element.7, bf16[1280,512]{0,1:T(8,128)(2,1)S(1)} %get-tuple-element.8), kind=kOutput, calls=%fused_computation.7 | convolution fusion | flops 10747904000 | bytes 21495808 | tf_op jit(solution)/shard_map/dot_general | solution.py:23
  593.7 15.2 %reshape.110 = bf16[128,10,4096]{2,1,0:T(8,128)(2,1)} reshape(bf16[1280,4096]{1,0:T(8,128)(2,1)} %convolution_convert_fusion) | data formatting | bytes 20971520 | tf_op jit(solution)/shard_map/reshape | solution.py:70
  608.8 10.2 %all-to-all-start.2 = ((bf16[128,10,4096]{2,1,0:T(8,128)(2,1)}), bf16[128,10,4096]{2,1,0:T(8,128)(2,1)}, u32[]{:S(2)}, u32[]{:S(2)}) async-start(bf16[128,10,4096]{2,1,0:T(8,128)(2,1)} %reshape.110), calls=%async_computation.2 | async-start | bytes 33554432 | tf_op jit(solution)/shard_map/all_to_all | solution.py:73
  619.5 6.8 gather_fusion.3
  627.1 229.1 %all-to-all-done.2 = bf16[128,10,4096]{2,1,0:T(8,128)(2,1)} async-done(((bf16[128,10,4096]{2,1,0:T(8,128)(2,1)}), bf16[128,10,4096]{2,1,0:T(8,128)(2,1)}, u32[]{:S(2)}, u32[]{:S(2)}) %all-to-all-start.2) | async-done | bytes 10485792 | tf_op jit(solution)/shard_map/all_to_all | solution.py:73
  856.2 16.5 %reshape.111 = bf16[1280,4096]{1,0:T(8,128)(2,1)} reshape(bf16[128,10,4096]{2,1,0:T(8,128)(2,1)} %all-to-all-done.2) | data formatting | bytes 20971520 | tf_op jit(solution)/shard_map/reshape | solution.py:79
  872.7 20.4 %gather_fusion.2 = bf16[1024,4096]{1,0:T(8,128)(2,1)} fusion(bf16[1280,4096]{1,0:T(8,128)(2,1)} %reshape.111, s32[1024]{0:T(1024)S(1)} %broadcast_clamp_fusion), kind=kCustom, calls=%fused_computation.2 | custom fusion | bytes 16781312 | tf_op jit(solution)/shard_map/gather | solution.py:79
  893.1 12.9 %fusion = bf16[128,4096]{1,0:T(8,128)(2,1)} fusion(bf16[1024,4096]{1,0:T(8,128)(2,1)} %gather_fusion.2, f32[128,8]{1,0:T(8,128)S(1)} %copy.23), kind=kLoop, calls=%fused_computation.6 | loop fusion | flops 12058624 | bytes 9441280 | tf_op jit(solution)/shard_map/reduce_sum | solution.py:84
  (38 shorter events, 4.9 us)
Async XLA Ops:
  3.4 0.6 copy-start.1
  33.2 12.6 %copy-start.4 = (s32[128]{0:T(128)S(1)}, s32[128]{0:T(128)}, u32[]{:S(2)}) copy-start(s32[128]{0:T(128)} %param.13) | copy-start | bytes 1540
  33.2 12.7 %copy-start = (bf16[128,4096]{1,0:T(8,128)(2,1)S(1)}, bf16[128,4096]{1,0:T(8,128)(2,1)}, u32[]{:S(2)}) copy-start(bf16[128,4096]{1,0:T(8,128)(2,1)} %param.9) | copy-start | bytes 3145732
  33.2 249.1 %all-to-all-start.1 = ((bf16[128,10,4096]{2,1,0:T(8,128)(2,1)}), bf16[128,10,4096]{2,1,0:T(8,128)(2,1)}, u32[]{:S(2)}, u32[]{:S(2)}) async-start(bf16[128,10,4096]{2,1,0:T(8,128)(2,1)} %reshape.108), calls=%async_computation.1 | async-start | bytes 33554432 | tf_op jit(solution)/shard_map/all_to_all | solution.py:56
  282.3 252.6 %all-to-all-start = ((bf16[128,10,4096]{2,1,0:T(8,128)(2,1)}), bf16[128,10,4096]{2,1,0:T(8,128)(2,1)}, u32[]{:S(2)}, u32[]{:S(2)}) async-start(bf16[128,10,4096]{2,1,0:T(8,128)(2,1)} %reshape.106), calls=%async_computation | async-start | bytes 33554432 | tf_op jit(solution)/shard_map/all_to_all | solution.py:63
  564.9 44.0 %all-to-all-start.3 = ((bf16[128,1,10]{2,1,0:T(2,128)(2,1)}), bf16[128,1,10]{2,1,0:T(2,128)(2,1)S(1)}, u32[]{:S(2)}, u32[]{:S(2)}) async-start(bf16[128,1,10]{2,1,0:T(2,128)(2,1)} %convert_element_type.62), calls=%async_computation.3 | async-start | bytes 131072 | tf_op jit(solution)/shard_map/all_to_all | solution.py:76
  608.8 10.2 %copy-start.3 = (f32[128,8]{0,1:T(8,128)S(1)}, f32[128,8]{0,1:T(8,128)}, u32[]{:S(2)}) copy-start(f32[128,8]{0,1:T(8,128)} %param.10) | copy-start | bytes 12292
  608.8 10.4 %copy-start.2 = (s32[1024,1]{0,1:T(1,128)S(1)}, s32[1024,1]{0,1:T(1,128)}, u32[]{:S(2)}) copy-start(s32[1024,1]{0,1:T(1,128)} %copy-done.1) | copy-start | bytes 12292
  608.8 247.4 %all-to-all-start.2 = ((bf16[128,10,4096]{2,1,0:T(8,128)(2,1)}), bf16[128,10,4096]{2,1,0:T(8,128)(2,1)}, u32[]{:S(2)}, u32[]{:S(2)}) async-start(bf16[128,10,4096]{2,1,0:T(8,128)(2,1)} %reshape.110), calls=%async_computation.2 | async-start | bytes 33554432 | tf_op jit(solution)/shard_map/all_to_all | solution.py:73
where the time goes:
time: 911 us; the launch traced here: 906 us
  waiting for transfers between devices  646 us (71%)
  local copies, waits for them, and re-layouts  149 us (16%)
  starting transfers between devices  48 us (5%)
  matrix products  47.3 us (5%)
  other arithmetic  14.7 us (2%)
    all_to_all x1, waiting for transfers between devices, body(): lax.all_to_all(row_grads, ('node', 'local'), split_axis=0, concat_axis=0,...  229 us
    all_to_all x1, waiting for transfers between devices, body(): lax.all_to_all(send_tokens, ('node', 'local'), split_axis=0, concat_axis=...  213 us
    all_to_all x1, waiting for transfers between devices, body(): lax.all_to_all(send_upstream, ('node', 'local'), split_axis=0, concat_axi...  204 us
    gather x1, local copies, waits for them, and re-layouts, body(): pair_grads = home_grads.reshape(device_count * capacity, width)[placed]  20.4 us
  transfers between devices with their start and end apart: 4, of which 3 were waited for; matrix products, arithmetic and copies ran while one was open for 11% of the time, Pallas kernels for 0%

commit v1 on v0

--- a/solution.py
+++ b/solution.py
@@ -49,15 +49,17 @@
     token_index = owner_table // chosen_count
     padded_tokens = jnp.concatenate([tokens, jnp.zeros((1, width), jnp.bfloat16)], axis=0)
     padded_upstream = jnp.concatenate([upstream, jnp.zeros((1, width), jnp.bfloat16)], axis=0)
-    send_tokens = padded_tokens[token_index].reshape(device_count, capacity, width)
-    send_upstream = padded_upstream[token_index].reshape(device_count, capacity, width)
+    block_rows = 16 if (capacity * width) % (16 * 128) == 0 else capacity
+    block = (device_count, block_rows, capacity * width // block_rows)
+    send_tokens = padded_tokens[token_index].reshape(block)
+    send_upstream = padded_upstream[token_index].reshape(block)
     weight_in = w_gate_up[0]
     weight_out = w_down[0]
     arrived_tokens = lax.all_to_all(
         send_tokens, ("node", "local"), split_axis=0, concat_axis=0, tiled=True
     )
     sources = arrived_tokens.shape[0]
-    items = arrived_tokens.shape[1]
+    items = capacity
     row_grads, prob_grad = expert_grads(
         arrived_tokens.reshape(sources * items, width),
         lax.all_to_all(
@@ -67,7 +69,7 @@
         weight_out,
     )
     row_grads, prob_grad = (
-        row_grads.reshape(sources, items, width),
+        row_grads.reshape(block),
         prob_grad.reshape(sources, items),
     )
     home_grads = lax.all_to_all(

time: 911 us -> 606 us (0.67)
  the two profiles are of different devices: /device:TPU:1 before, /device:TPU:4 now
where the time goes in v1:
time: 606 us; the launch traced here: 597 us
  waiting for transfers between devices  336 us (55%)
  local copies, waits for them, and re-layouts  166 us (27%)
  matrix products  47.2 us (8%)
  starting transfers between devices  30.9 us (5%)
  other arithmetic  14.7 us (2%)
    all_to_all x1, waiting for transfers between devices, body(): lax.all_to_all(row_grads, ('node', 'local'), split_axis=0, concat_axis=0,...  129 us
    all_to_all x1, waiting for transfers between devices, body(): lax.all_to_all(send_tokens, ('node', 'local'), split_axis=0, concat_axis=...  109 us
    all_to_all x1, waiting for transfers between devices, body(): lax.all_to_all(send_upstream, ('node', 'local'), split_axis=0, concat_axi...  98.5 us
    gather x1, local copies, waits for them, and re-layouts, body(): pair_grads = home_grads.reshape(device_count * capacity, width)[placed]  20.6 us
    reshape x1, local copies, waits for them, and re-layouts, body(): arrived_tokens.reshape(sources * items, width)  18.7 us
    reshape x1, local copies, waits for them, and re-layouts, body(): pair_grads = home_grads.reshape(device_count * capacity, width)[placed]  18.7 us
    reshape x1, local copies, waits for them, and re-layouts, body(): row_grads, prob_grad = expert_grads(arrived_tokens.reshape(sources * item...  18.7 us
    reshape x1, local copies, waits for them, and re-layouts, body(): send_tokens = padded_tokens[token_index].reshape(block)  18.7 us
  transfers between devices with their start and end apart: 4, of which 3 were waited for; matrix products, arithmetic and copies ran while one was open for 18% of the time, Pallas kernels for 0%

profile of v1, /device:TPU:4, one launch (start us, length us, event | category | flops | bytes accessed | tf_op | source)
XLA Modules:
  0.0 597.0 jit_solution(5254290708059599130)
XLA Ops:
  4.0 4.3 scatter_custom_fusion
  8.3 1.3 concatenate.11
  9.7 8.4 %gather_fusion.1 = bf16[1280,4096]{1,0:T(8,128)(2,1)} fusion(bf16[129,4096]{1,0:T(8,128)(2,1)S(1)} %concatenate.11, s32[2048]{0:T(1024)S(1)} %pad_clamp_fusion), kind=kCustom, calls=%fused_computation.1 | custom fusion | bytes 20976640 | tf_op jit(solution)/shard_map/gather | solution.py:54
  18.0 18.7 %reshape.108 = bf16[128,16,2560]{2,1,0:T(8,128)(2,1)} reshape(bf16[1280,4096]{1,0:T(8,128)(2,1)} %gather_fusion.1) | data formatting | bytes 20971520 | tf_op jit(solution)/shard_map/reshape | solution.py:54
  36.7 10.9 %all-to-all-start.1 = ((bf16[128,16,2560]{2,1,0:T(8,128)(2,1)}), bf16[128,16,2560]{2,1,0:T(8,128)(2,1)}, u32[]{:S(2)}, u32[]{:S(2)}) async-start(bf16[128,16,2560]{2,1,0:T(8,128)(2,1)} %reshape.108), calls=%async_computation.1 | async-start | bytes 20971520 | tf_op jit(solution)/shard_map/all_to_all | solution.py:58
  48.7 8.3 %gather_fusion = bf16[1280,4096]{1,0:T(8,128)(2,1)} fusion(bf16[129,4096]{1,0:T(8,128)(2,1)S(1)} %concatenate.10, s32[2048]{0:T(1024)S(1)} %pad_clamp_fusion), kind=kCustom, calls=%fused_computation | custom fusion | bytes 20976640 | tf_op jit(solution)/shard_map/gather | solution.py:55
  57.0 18.7 %reshape.106 = bf16[128,16,2560]{2,1,0:T(8,128)(2,1)} reshape(bf16[1280,4096]{1,0:T(8,128)(2,1)} %gather_fusion) | data formatting | bytes 20971520 | tf_op jit(solution)/shard_map/reshape | solution.py:55
  75.7 109.0 %all-to-all-done.1 = bf16[128,16,2560]{2,1,0:T(8,128)(2,1)} async-done(((bf16[128,16,2560]{2,1,0:T(8,128)(2,1)}), bf16[128,16,2560]{2,1,0:T(8,128)(2,1)}, u32[]{:S(2)}, u32[]{:S(2)}) %all-to-all-start.1) | async-done | bytes 10485792 | tf_op jit(solution)/shard_map/all_to_all | solution.py:58
  184.6 5.1 all-to-all-start
  189.8 18.7 %reshape.109 = bf16[1280,4096]{1,0:T(8,128)(2,1)} reshape(bf16[128,16,2560]{2,1,0:T(8,128)(2,1)} %all-to-all-done.1) | data formatting | bytes 20971520 | tf_op jit(solution)/shard_map/reshape | solution.py:64
  208.5 17.4 %fusion.2 = f32[1280,1024]{0,1:T(8,128)} fusion(bf16[1280,4096]{1,0:T(8,128)(2,1)} %reshape.109, bf16[1,4096,1024]{2,1,0:T(8,128)(2,1)} %param.14), kind=kOutput, calls=%fused_computation.9 | convolution fusion | flops 10737418240 | bytes 24117248 | tf_op jit(solution)/shard_map/dot_general | solution.py:12
  225.9 98.5 %all-to-all-done = bf16[128,16,2560]{2,1,0:T(8,128)(2,1)} async-done(((bf16[128,16,2560]{2,1,0:T(8,128)(2,1)}), bf16[128,16,2560]{2,1,0:T(8,128)(2,1)}, u32[]{:S(2)}, u32[]{:S(2)}) %all-to-all-start) | async-done | bytes 10485792 | tf_op jit(solution)/shard_map/all_to_all | solution.py:65
  324.4 18.7 %reshape.107 = bf16[1280,4096]{1,0:T(8,128)(2,1)} reshape(bf16[128,16,2560]{2,1,0:T(8,128)(2,1)} %all-to-all-done) | data formatting | bytes 20971520 | tf_op jit(solution)/shard_map/reshape | solution.py:67
  343.1 12.7 %multiply_reduce_fusion = (bf16[1280]{0:T(1024)(128)(2,1)S(1)}, bf16[1280,512]{0,1:T(8,128)(2,1)S(1)}, bf16[1280,512]{0,1:T(8,128)(2,1)S(1)}) fusion(f32[1280,1024]{0,1:T(8,128)} %fusion.2, bf16[1280,4096]{1,0:T(8,128)(2,1)} %reshape.107, bf16[1,512,4096]{2,1,0:T(8,128)(2,1)} %param.15), kind=kOutput, calls=%fused_computation.16 | convolution fusion | flops 5380504576 | bytes 22546944 | tf_op jit(solution)/shard_map/dot_general | solution.py:18
  355.8 0.8 convert_element_type.62
  356.6 4.7 all-to-all-start.3
  361.3 17.1 %convolution_convert_fusion = bf16[1280,4096]{1,0:T(8,128)(2,1)} fusion(bf16[1,4096,1024]{2,1,0:T(8,128)(2,1)} %param.14, bf16[1280,512]{0,1:T(8,128)(2,1)S(1)} %get-tuple-element.7, bf16[1280,512]{0,1:T(8,128)(2,1)S(1)} %get-tuple-element.8), kind=kOutput, calls=%fused_computation.7 | convolution fusion | flops 10747904000 | bytes 21495808 | tf_op jit(solution)/shard_map/dot_general | solution.py:23
  378.4 18.7 %reshape.110 = bf16[128,16,2560]{2,1,0:T(8,128)(2,1)} reshape(bf16[1280,4096]{1,0:T(8,128)(2,1)} %convolution_convert_fusion) | data formatting | bytes 20971520 | tf_op jit(solution)/shard_map/reshape | solution.py:72
  397.1 10.2 %all-to-all-start.2 = ((bf16[128,16,2560]{2,1,0:T(8,128)(2,1)}), bf16[128,16,2560]{2,1,0:T(8,128)(2,1)}, u32[]{:S(2)}, u32[]{:S(2)}) async-start(bf16[128,16,2560]{2,1,0:T(8,128)(2,1)} %reshape.110), calls=%async_computation.2 | async-start | bytes 20971520 | tf_op jit(solution)/shard_map/all_to_all | solution.py:75
  407.8 6.8 %gather_fusion.3 = bf16[1024]{0:T(1024)(128)(2,1)S(1)} fusion(bf16[1280]{0:T(1024)(128)(2,1)S(1)} %reshape.112, s32[1024]{0:T(1024)S(1)} %broadcast_clamp_fusion), kind=kCustom, calls=%fused_computation.3 | custom fusion | bytes 8192 | tf_op jit(solution)/shard_map/gather | solution.py:87
  415.3 129.0 %all-to-all-done.2 = bf16[128,16,2560]{2,1,0:T(8,128)(2,1)} async-done(((bf16[128,16,2560]{2,1,0:T(8,128)(2,1)}), bf16[128,16,2560]{2,1,0:T(8,128)(2,1)}, u32[]{:S(2)}, u32[]{:S(2)}) %all-to-all-start.2) | async-done | bytes 10485792 | tf_op jit(solution)/shard_map/all_to_all | solution.py:75
  544.3 18.7 %reshape.111 = bf16[1280,4096]{1,0:T(8,128)(2,1)} reshape(bf16[128,16,2560]{2,1,0:T(8,128)(2,1)} %all-to-all-done.2) | data formatting | bytes 20971520 | tf_op jit(solution)/shard_map/reshape | solution.py:81
  563.0 20.6 %gather_fusion.2 = bf16[1024,4096]{1,0:T(8,128)(2,1)} fusion(bf16[1280,4096]{1,0:T(8,128)(2,1)} %reshape.111, s32[1024]{0:T(1024)S(1)} %broadcast_clamp_fusion), kind=kCustom, calls=%fused_computation.2 | custom fusion | bytes 16781312 | tf_op jit(solution)/shard_map/gather | solution.py:81
  583.7 12.9 %fusion = bf16[128,4096]{1,0:T(8,128)(2,1)} fusion(bf16[1024,4096]{1,0:T(8,128)(2,1)} %gather_fusion.2, f32[128,8]{1,0:T(8,128)S(1)} %copy.23), kind=kLoop, calls=%fused_computation.6 | loop fusion | flops 12058624 | bytes 9441280 | tf_op jit(solution)/shard_map/reduce_sum | solution.py:86
  (38 shorter events, 4.9 us)
Async XLA Ops:
  3.4 0.6 copy-start.1
  36.7 11.6 %copy-start.4 = (s32[128]{0:T(128)S(1)}, s32[128]{0:T(128)}, u32[]{:S(2)}) copy-start(s32[128]{0:T(128)} %param.13) | copy-start | bytes 1540
  36.7 11.6 %copy-start = (bf16[128,4096]{1,0:T(8,128)(2,1)S(1)}, bf16[128,4096]{1,0:T(8,128)(2,1)}, u32[]{:S(2)}) copy-start(bf16[128,4096]{1,0:T(8,128)(2,1)} %param.9) | copy-start | bytes 3145732
  36.7 147.9 %all-to-all-start.1 = ((bf16[128,16,2560]{2,1,0:T(8,128)(2,1)}), bf16[128,16,2560]{2,1,0:T(8,128)(2,1)}, u32[]{:S(2)}, u32[]{:S(2)}) async-start(bf16[128,16,2560]{2,1,0:T(8,128)(2,1)} %reshape.108), calls=%async_computation.1 | async-start | bytes 20971520 | tf_op jit(solution)/shard_map/all_to_all | solution.py:58
  184.6 139.8 %all-to-all-start = ((bf16[128,16,2560]{2,1,0:T(8,128)(2,1)}), bf16[128,16,2560]{2,1,0:T(8,128)(2,1)}, u32[]{:S(2)}, u32[]{:S(2)}) async-start(bf16[128,16,2560]{2,1,0:T(8,128)(2,1)} %reshape.106), calls=%async_computation | async-start | bytes 20971520 | tf_op jit(solution)/shard_map/all_to_all | solution.py:65
  356.6 40.5 %all-to-all-start.3 = ((bf16[128,1,10]{2,1,0:T(2,128)(2,1)}), bf16[128,1,10]{2,1,0:T(2,128)(2,1)S(1)}, u32[]{:S(2)}, u32[]{:S(2)}) async-start(bf16[128,1,10]{2,1,0:T(2,128)(2,1)} %convert_element_type.62), calls=%async_computation.3 | async-start | bytes 131072 | tf_op jit(solution)/shard_map/all_to_all | solution.py:78
  397.1 10.2 %copy-start.3 = (f32[128,8]{0,1:T(8,128)S(1)}, f32[128,8]{0,1:T(8,128)}, u32[]{:S(2)}) copy-start(f32[128,8]{0,1:T(8,128)} %param.10) | copy-start | bytes 12292
  397.1 10.3 %copy-start.2 = (s32[1024,1]{0,1:T(1,128)S(1)}, s32[1024,1]{0,1:T(1,128)}, u32[]{:S(2)}) copy-start(s32[1024,1]{0,1:T(1,128)} %copy-done.1) | copy-start | bytes 12292
  397.1 147.2 %all-to-all-start.2 = ((bf16[128,16,2560]{2,1,0:T(8,128)(2,1)}), bf16[128,16,2560]{2,1,0:T(8,128)(2,1)}, u32[]{:S(2)}, u32[]{:S(2)}) async-start(bf16[128,16,2560]{2,1,0:T(8,128)(2,1)} %reshape.110), calls=%async_computation.2 | async-start | bytes 20971520 | tf_op jit(solution)/shard_map/all_to_all | solution.py:75

commit v2 on v0

--- a/solution.py
+++ b/solution.py
@@ -27,7 +27,8 @@
 
 
 def body(tokens, cotangent, gate_probs, experts, stratum, token_level, w_gate_up, w_down):
-    device_count = lax.axis_size(("node", "local"))
+    axes = ("node", "local")
+    device_count = lax.axis_size(axes)
     token_rows, chosen_count = experts.shape
     width = tokens.shape[1]
     capacity = max(2, token_rows * chosen_count * 5 // (4 * device_count))
@@ -46,44 +47,79 @@
     placed = chosen * capacity + ranking
     owner_table = jnp.full((device_count * capacity,), pair_count, jnp.int32)
     owner_table = owner_table.at[placed].set(jnp.arange(pair_count, dtype=jnp.int32))
-    token_index = owner_table // chosen_count
+    token_index = (owner_table // chosen_count).reshape(device_count, capacity)
     padded_tokens = jnp.concatenate([tokens, jnp.zeros((1, width), jnp.bfloat16)], axis=0)
     padded_upstream = jnp.concatenate([upstream, jnp.zeros((1, width), jnp.bfloat16)], axis=0)
-    send_tokens = padded_tokens[token_index].reshape(device_count, capacity, width)
-    send_upstream = padded_upstream[token_index].reshape(device_count, capacity, width)
     weight_in = w_gate_up[0]
     weight_out = w_down[0]
-    arrived_tokens = lax.all_to_all(
-        send_tokens, ("node", "local"), split_axis=0, concat_axis=0, tiled=True
-    )
-    sources = arrived_tokens.shape[0]
-    items = arrived_tokens.shape[1]
-    row_grads, prob_grad = expert_grads(
-        arrived_tokens.reshape(sources * items, width),
-        lax.all_to_all(
-            send_upstream, ("node", "local"), split_axis=0, concat_axis=0, tiled=True
-        ).reshape(sources * items, width),
-        weight_in,
-        weight_out,
-    )
-    row_grads, prob_grad = (
-        row_grads.reshape(sources, items, width),
-        prob_grad.reshape(sources, items),
-    )
-    home_grads = lax.all_to_all(
-        row_grads, ("node", "local"), split_axis=0, concat_axis=0, tiled=True
-    )
-    home_probs = lax.all_to_all(
-        prob_grad, ("node", "local"), split_axis=0, concat_axis=0, tiled=True
-    )
-    pair_grads = home_grads.reshape(device_count * capacity, width)[placed]
-    weighted = (
-        pair_grads.astype(jnp.float32).reshape(token_rows, chosen_count, width)
-        * gate_probs[:, :, None]
-    )
-    grad_tokens = jnp.sum(weighted, axis=1).astype(jnp.bfloat16)
-    grad_probs = home_probs.reshape(-1)[placed].reshape(token_rows, chosen_count)
-    return (grad_tokens, grad_probs)
+    chunks = 2 if capacity % 2 == 0 else 1
+    per_chunk = capacity // chunks
+    block_rows = 16 if (per_chunk * width) % (16 * 128) == 0 else per_chunk
+    block = (device_count, block_rows, per_chunk * width // block_rows)
+    chunk_slots = device_count * per_chunk
+    def exchange(part):
+        return lax.all_to_all(part, axes, 0, 0, tiled=True)
+
+    def send_of(c):
+        index = token_index[:, c * per_chunk : (c + 1) * per_chunk].reshape(-1)
+        return jnp.concatenate(
+            [padded_tokens[index].reshape(block), padded_upstream[index].reshape(block)], axis=1
+        )
+
+    def compute(arrived):
+        row_grads, prob_grad = expert_grads(
+            arrived[:, :block_rows].reshape(chunk_slots, width),
+            arrived[:, block_rows:].reshape(chunk_slots, width),
+            weight_in,
+            weight_out,
+        )
+        return row_grads.reshape(block), prob_grad.reshape(device_count, 1, per_chunk)
+
+    def combine(c, home):
+        local = ranking - c * per_chunk
+        inside = (local >= 0) & (local < per_chunk)
+        slot = jnp.where(inside, chosen * per_chunk + local, -1).reshape(token_rows, chosen_count)
+        weight = jnp.where(inside.reshape(token_rows, chosen_count), gate_probs, 0.0)
+        table = jnp.sum(
+            jnp.where(
+                slot[:, :, None] == jnp.arange(chunk_slots, dtype=jnp.int32)[None, None, :],
+                weight[:, :, None],
+                0.0,
+            ),
+            axis=1,
+        )
+        high = table.astype(jnp.bfloat16)
+        low = (table - high.astype(jnp.float32)).astype(jnp.bfloat16)
+        home = home.reshape(chunk_slots, width)
+        return jnp.dot(high, home, preferred_element_type=jnp.float32) + jnp.dot(
+            low, home, preferred_element_type=jnp.float32
+        )
+
+    arrived = exchange(send_of(0))
+    grad_tokens = None
+    prob_parts = []
+    pending = None
+    for c in range(chunks):
+        row_grads, prob_grad = compute(arrived)
+        if c + 1 < chunks:
+            arrived = exchange(send_of(c + 1))
+            arrived, row_grads, prob_grad = lax.optimization_barrier(
+                (arrived, row_grads, prob_grad)
+            )
+        if pending is not None:
+            pending, row_grads, prob_grad = lax.optimization_barrier(
+                (pending, row_grads, prob_grad)
+            )
+            part = combine(c - 1, pending[0])
+            prob_parts.append(pending[1].reshape(device_count, per_chunk))
+            grad_tokens = part if grad_tokens is None else grad_tokens + part
+        pending = (exchange(row_grads), exchange(prob_grad))
+    part = combine(chunks - 1, pending[0])
+    prob_parts.append(pending[1].reshape(device_count, per_chunk))
+    grad_tokens = part if grad_tokens is None else grad_tokens + part
+    home_probs = jnp.concatenate(prob_parts, axis=1).reshape(-1)
+    grad_probs = home_probs[placed].reshape(token_rows, chosen_count)
+    return (grad_tokens.astype(jnp.bfloat16), grad_probs)
 
 
 def solution(mesh):

time: 911 us -> 537 us (0.59)
  waiting for transfers between devices: 646 us -> 197 us
  blocking collectives: 0 us -> 36 us
  local copies, waits for them, and re-layouts: 149 us -> 175 us
  starting transfers between devices: 48 us -> 32.5 us
  matrix products: 47.3 us -> 59.9 us
  other arithmetic: 14.7 us -> 26.4 us
    all_to_all x4, waiting for transfers between devices: 646 us -> 197 us  [exchange(): return lax.all_to_all(part, axes, 0, 0, tiled=True)]
    all_to_all x0 -> x2, blocking collectives: none -> 36 us  [exchange(): return lax.all_to_all(part, axes, 0, 0, tiled=True)]
    reshape x8 -> x17, local copies, waits for them, and re-layouts: 95.4 us -> 120 us  [the longest x2 19.9 us: compute(): arrived[:, :block_rows].reshape(chunk_slots, width)]
    concatenate x0 -> x3, other arithmetic: none -> 20.5 us  [the longest x2 20.5 us: send_of(): jnp.concatenate([padded_tokens[index].reshape(block), padded_upstream[ind...]
    slice x0 -> x3, local copies, waits for them, and re-layouts: none -> 17.4 us  [the longest x2 17.3 us: compute(): arrived[:, :block_rows].reshape(chunk_slots, width)]
    gather x4 -> x5, local copies, waits for them, and re-layouts: 43.8 us -> 28.2 us  [the longest x2 10.7 us: send_of(): padded_tokens[index].reshape(block)]
    all_to_all x4, starting transfers between devices: 48 us -> 32.5 us  [exchange(): return lax.all_to_all(part, axes, 0, 0, tiled=True)]
    reduce_sum x1, other arithmetic: 12.9 us -> 1.72 us  [combine(): jnp.sum(jnp.where(slot[:, :, None] == jnp.arange(chunk_slots, dtype=jnp.i...]
  transfers between devices with their start and end apart: 4 -> 4, of which waited for: 3 -> 4; matrix products, arithmetic and copies ran while one was open for 11% -> 36% of each run, Pallas kernels for 0% -> 0%
where the time goes in v2:
time: 537 us; the launch traced here: 528 us
  waiting for transfers between devices  197 us (37%)
  local copies, waits for them, and re-layouts  175 us (33%)
  matrix products  59.9 us (11%)
  blocking collectives  36 us (7%)
  starting transfers between devices  32.5 us (6%)
  other arithmetic  26.4 us (5%)
    all_to_all x4, waiting for transfers between devices, exchange(): return lax.all_to_all(part, axes, 0, 0, tiled=True)  197 us
    all_to_all x2, blocking collectives, exchange(): return lax.all_to_all(part, axes, 0, 0, tiled=True)  36 us
    all_to_all x4, starting transfers between devices, exchange(): return lax.all_to_all(part, axes, 0, 0, tiled=True)  32.5 us
    dot_general x2, matrix products, expert_grads(): projected = jnp.dot(inputs, weight_in, preferred_element_type=jnp.float32)  21.9 us
    concatenate x2, other arithmetic, send_of(): jnp.concatenate([padded_tokens[index].reshape(block), padded_upstream[ind...  20.5 us
    reshape x2, local copies, waits for them, and re-layouts, compute(): arrived[:, :block_rows].reshape(chunk_slots, width)  19.9 us
    dot_general x2, matrix products, expert_grads(): jnp.dot(stacked, weight_in.T, preferred_element_type=jnp.float32)  19.9 us
    reshape x2, local copies, waits for them, and re-layouts, send_of(): padded_upstream[index].reshape(block)  19.9 us
  transfers between devices with their start and end apart: 4, of which 4 were waited for; matrix products, arithmetic and copies ran while one was open for 36% of the time, Pallas kernels for 0%

profile of v2, /device:TPU:1, one launch (start us, length us, event | category | flops | bytes accessed | tf_op | source)
XLA Modules:
  0.0 528.4 jit_solution(6921538821162381666)
XLA Ops:
  17.7 10.0 %reshape.232 = bf16[128,16,1280]{2,1,0:T(8,128)(2,1)} reshape(bf16[640,4096]{1,0:T(8,128)(2,1)} %gather_fusion.3) | data formatting | bytes 10485760 | tf_op jit(solution)/shard_map/reshape | solution.py:66
  33.1 9.9 %reshape.231 = bf16[128,16,1280]{2,1,0:T(8,128)(2,1)} reshape(bf16[640,4096]{1,0:T(8,128)(2,1)} %gather_fusion.2) | data formatting | bytes 10485760 | tf_op jit(solution)/shard_map/reshape | solution.py:66
  43.0 10.3 %pad_maximum_fusion.1 = bf16[128,32,1280]{2,1,0:T(8,128)(2,1)} fusion(bf16[128,16,1280]{2,1,0:T(8,128)(2,1)} %reshape.232, bf16[128,16,1280]{2,1,0:T(8,128)(2,1)} %reshape.231), kind=kLoop, calls=%fused_computation.7 | loop fusion | flops 20971520 | bytes 20971520 | tf_op jit(solution)/shard_map/concatenate | solution.py:65
  53.3 12.3 %all-to-all-start.1 = ((bf16[128,32,1280]{2,1,0:T(8,128)(2,1)}), bf16[128,32,1280]{2,1,0:T(8,128)(2,1)}, u32[]{:S(2)}, u32[]{:S(2)}) async-start(bf16[128,32,1280]{2,1,0:T(8,128)(2,1)} %pad_maximum_fusion.1), calls=%async_computation.1 | async-start | bytes 20971520 | tf_op jit(solution)/shard_map/all_to_all | solution.py:61
  76.5 9.9 %reshape.229 = bf16[128,16,1280]{2,1,0:T(8,128)(2,1)} reshape(bf16[640,4096]{1,0:T(8,128)(2,1)} %gather_fusion.1) | data formatting | bytes 10485760 | tf_op jit(solution)/shard_map/reshape | solution.py:66
  86.4 9.9 %reshape.228 = bf16[128,16,1280]{2,1,0:T(8,128)(2,1)} reshape(bf16[640,4096]{1,0:T(8,128)(2,1)} %gather_fusion) | data formatting | bytes 10485760 | tf_op jit(solution)/shard_map/reshape | solution.py:66
  96.3 10.2 %pad_maximum_fusion = bf16[128,32,1280]{2,1,0:T(8,128)(2,1)} fusion(bf16[128,16,1280]{2,1,0:T(8,128)(2,1)} %reshape.229, bf16[128,16,1280]{2,1,0:T(8,128)(2,1)} %reshape.228), kind=kLoop, calls=%fused_computation.6 | loop fusion | flops 20971520 | bytes 20971520 | tf_op jit(solution)/shard_map/concatenate | solution.py:65
  106.5 90.7 %all-to-all-done.1 = bf16[128,32,1280]{2,1,0:T(8,128)(2,1)} async-done(((bf16[128,32,1280]{2,1,0:T(8,128)(2,1)}), bf16[128,32,1280]{2,1,0:T(8,128)(2,1)}, u32[]{:S(2)}, u32[]{:S(2)}) %all-to-all-start.1) | async-done | bytes 10485792 | tf_op jit(solution)/shard_map/all_to_all | solution.py:61
  214.2 10.0 %reshape.234 = bf16[640,4096]{1,0:T(8,128)(2,1)} reshape(bf16[128,16,1280]{2,1,0:T(8,128)(2,1)} %get-tuple-element.26) | data formatting | bytes 10485760 | tf_op jit(solution)/shard_map/reshape | solution.py:71
  224.2 9.9 %reshape.233 = bf16[640,4096]{1,0:T(8,128)(2,1)} reshape(bf16[128,16,1280]{2,1,0:T(8,128)(2,1)} %get-tuple-element.27) | data formatting | bytes 10485760 | tf_op jit(solution)/shard_map/reshape | solution.py:72
  234.1 10.9 %fusion.6 = f32[640,1024]{0,1:T(8,128)S(1)} fusion(bf16[640,4096]{1,0:T(8,128)(2,1)} %reshape.234, bf16[1,4096,1024]{2,1,0:T(8,128)(2,1)} %param.14), kind=kOutput, calls=%fused_computation.14 | convolution fusion | flops 5368709120 | bytes 16252928 | tf_op jit(solution)/shard_map/dot_general | solution.py:12
  249.0 10.1 %fusion.8 = bf16[640,4096]{1,0:T(8,128)(2,1)} fusion(bf16[1,4096,1024]{2,1,0:T(8,128)(2,1)} %param.14, bf16[640,512]{0,1:T(8,128)(2,1)S(1)} %get-tuple-element.32, bf16[640,512]{0,1:T(8,128)(2,1)S(1)} %get-tuple-element.33), kind=kOutput, calls=%fused_computation.16 | convolution fusion | flops 5373952000 | bytes 14942208 | tf_op jit(solution)/shard_map/dot_general | solution.py:23
  259.1 10.0 %reshape.235 = bf16[128,16,1280]{2,1,0:T(8,128)(2,1)} reshape(bf16[640,4096]{1,0:T(8,128)(2,1)} %fusion.8) | data formatting | bytes 10485760 | tf_op jit(solution)/shard_map/reshape | solution.py:76
  269.3 67.8 %all-to-all-done = bf16[128,32,1280]{2,1,0:T(8,128)(2,1)} async-done(((bf16[128,32,1280]{2,1,0:T(8,128)(2,1)}), bf16[128,32,1280]{2,1,0:T(8,128)(2,1)}, u32[]{:S(2)}, u32[]{:S(2)}) %all-to-all-start) | async-done | bytes 10485792 | tf_op jit(solution)/shard_map/all_to_all | solution.py:61
  337.1 16.8 %all_to_all.30 = bf16[128,1,5]{2,1,0:T(2,128)(2,1)S(1)} all-to-all(bf16[128,1,5]{2,1,0:T(2,128)(2,1)S(1)} %copy.85), channel_id=1, replica_groups=mesh['node'=8,'local'=16] {'node','local'}, dimensions={0} | all-to-all | bytes 2560 | tf_op jit(solution)/shard_map/all_to_all | solution.py:61
  368.5 9.9 %reshape.237 = bf16[640,4096]{1,0:T(8,128)(2,1)} reshape(bf16[128,16,1280]{2,1,0:T(8,128)(2,1)} %get-tuple-element.24) | data formatting | bytes 10485760 | tf_op jit(solution)/shard_map/reshape | solution.py:71
  378.4 9.9 %reshape.236 = bf16[640,4096]{1,0:T(8,128)(2,1)} reshape(bf16[128,16,1280]{2,1,0:T(8,128)(2,1)} %get-tuple-element.25) | data formatting | bytes 10485760 | tf_op jit(solution)/shard_map/reshape | solution.py:72
  388.3 10.9 %fusion.2 = f32[640,1024]{0,1:T(8,128)S(1)} fusion(bf16[640,4096]{1,0:T(8,128)(2,1)} %reshape.237, bf16[1,4096,1024]{2,1,0:T(8,128)(2,1)} %param.14), kind=kOutput, calls=%fused_computation.10 | convolution fusion | flops 5368709120 | bytes 16252928 | tf_op jit(solution)/shard_map/dot_general | solution.py:12
  403.2 9.8 %fusion.11 = bf16[640,4096]{1,0:T(8,128)(2,1)} fusion(bf16[1,4096,1024]{2,1,0:T(8,128)(2,1)} %param.14, bf16[640,512]{0,1:T(8,128)(2,1)S(1)} %get-tuple-element.29, bf16[640,512]{0,1:T(8,128)(2,1)S(1)} %get-tuple-element.30), kind=kOutput, calls=%fused_computation.17 | convolution fusion | flops 5373952000 | bytes 14942208 | tf_op jit(solution)/shard_map/dot_general | solution.py:23
  413.1 9.9 %reshape.238 = bf16[128,16,1280]{2,1,0:T(8,128)(2,1)} reshape(bf16[640,4096]{1,0:T(8,128)(2,1)} %fusion.11) | data formatting | bytes 10485760 | tf_op jit(solution)/shard_map/reshape | solution.py:76
  423.4 19.2 %all_to_all.31 = bf16[128,1,5]{2,1,0:T(2,128)(2,1)S(1)} all-to-all(bf16[128,1,5]{2,1,0:T(2,128)(2,1)S(1)} %copy.91), channel_id=1, replica_groups=mesh['node'=8,'local'=16] {'node','local'}, dimensions={0} | all-to-all | bytes 2560 | tf_op jit(solution)/shard_map/all_to_all | solution.py:61
  450.8 9.9 %reshape.239 = bf16[640,4096]{1,0:T(8,128)(2,1)} reshape(bf16[128,16,1280]{2,1,0:T(8,128)(2,1)} %all-to-all-done.2) | data formatting | bytes 10485760 | tf_op jit(solution)/shard_map/reshape | solution.py:93
  473.8 38.3 %all-to-all-done.4 = bf16[128,16,1280]{2,1,0:T(8,128)(2,1)} async-done(((bf16[128,16,1280]{2,1,0:T(8,128)(2,1)}), bf16[128,16,1280]{2,1,0:T(8,128)(2,1)}, u32[]{:S(2)}, u32[]{:S(2)}) %all-to-all-start.4) | async-done | bytes 5242912 | tf_op jit(solution)/shard_map/all_to_all | solution.py:61
  512.1 9.9 %reshape.240 = bf16[640,4096]{1,0:T(8,128)(2,1)} reshape(bf16[128,16,1280]{2,1,0:T(8,128)(2,1)} %all-to-all-done.4) | data formatting | bytes 10485760 | tf_op jit(solution)/shard_map/reshape | solution.py:93
  (91 shorter events, 99.9 us)
Async XLA Ops:
  4.0 0.6 copy-start.5
  4.6 4.3 copy-start.8
  17.7 10.0 %copy-start.4 = (bf16[128,4096]{1,0:T(8,128)(2,1)S(1)}, bf16[128,4096]{1,0:T(8,128)(2,1)}, u32[]{:S(2)}) copy-start(bf16[128,4096]{1,0:T(8,128)(2,1)} %param.8) | copy-start | bytes 3145732
  53.3 143.9 %all-to-all-start.1 = ((bf16[128,32,1280]{2,1,0:T(8,128)(2,1)}), bf16[128,32,1280]{2,1,0:T(8,128)(2,1)}, u32[]{:S(2)}, u32[]{:S(2)}) async-start(bf16[128,32,1280]{2,1,0:T(8,128)(2,1)} %pad_maximum_fusion.1), calls=%async_computation.1 | async-start | bytes 20971520 | tf_op jit(solution)/shard_map/all_to_all | solution.py:61
  197.2 139.9 %all-to-all-start = ((bf16[128,32,1280]{2,1,0:T(8,128)(2,1)}), bf16[128,32,1280]{2,1,0:T(8,128)(2,1)}, u32[]{:S(2)}, u32[]{:S(2)}) async-start(bf16[128,32,1280]{2,1,0:T(8,128)(2,1)} %pad_maximum_fusion), calls=%async_computation | async-start | bytes 20971520 | tf_op jit(solution)/shard_map/all_to_all | solution.py:61
  234.1 11.0 %copy-start.2 = (bf16[640,4096]{1,0:T(8,128)(2,1)S(1)}, bf16[640,4096]{1,0:T(8,128)(2,1)}, u32[]{:S(2)}) copy-start(bf16[640,4096]{1,0:T(8,128)(2,1)} %reshape.233) | copy-start | bytes 15728644
  234.1 11.0 %copy-start.11 = (bf16[1,512,4096]{2,1,0:T(8,128)(2,1)S(1)}, bf16[1,512,4096]{2,1,0:T(8,128)(2,1)}, u32[]{:S(2)}) copy-start(bf16[1,512,4096]{2,1,0:T(8,128)(2,1)} %param.15) | copy-start | bytes 12582916
  354.0 69.4 %all-to-all-start.2 = ((bf16[128,16,1280]{2,1,0:T(8,128)(2,1)}), bf16[128,16,1280]{2,1,0:T(8,128)(2,1)}, u32[]{:S(2)}, u32[]{:S(2)}) async-start(bf16[128,16,1280]{2,1,0:T(8,128)(2,1)} %reshape.235), calls=%async_computation.2 | async-start | bytes 10485760 | tf_op jit(solution)/shard_map/all_to_all | solution.py:61
  388.3 11.0 %copy-start.3 = (bf16[640,4096]{1,0:T(8,128)(2,1)S(1)}, bf16[640,4096]{1,0:T(8,128)(2,1)}, u32[]{:S(2)}) copy-start(bf16[640,4096]{1,0:T(8,128)(2,1)} %reshape.236) | copy-start | bytes 15728644
  388.3 11.0 %copy-start.12 = (bf16[1,512,4096]{2,1,0:T(8,128)(2,1)S(1)}, bf16[1,512,4096]{2,1,0:T(8,128)(2,1)}, u32[]{:S(2)}) copy-start(bf16[1,512,4096]{2,1,0:T(8,128)(2,1)} %param.15) | copy-start | bytes 12582916
  442.5 6.1 %copy-start.6 = (s32[1024]{0:T(1024)S(1)}, s32[1024]{0:T(1024)}, u32[]{:S(2)}) copy-start(s32[1024]{0:T(1024)} %copy-done.5) | copy-start | bytes 12292
  442.5 6.2 %copy-start.7 = (s32[128,8]{0,1:T(8,128)S(1)}, s32[128,8]{0,1:T(8,128)}, u32[]{:S(2)}) copy-start(s32[128,8]{0,1:T(8,128)} %get-tuple-element.40) | copy-start | bytes 12292
  442.5 6.3 %copy-start.10 = (f32[128,8]{0,1:T(8,128)S(1)}, f32[128,8]{0,1:T(8,128)}, u32[]{:S(2)}) copy-start(f32[128,8]{0,1:T(8,128)} %param.10) | copy-start | bytes 12292
  442.5 6.4 %copy-start.9 = (s32[1024,1]{0,1:T(1,128)S(1)}, s32[1024,1]{0,1:T(1,128)}, u32[]{:S(2)}) copy-start(s32[1024,1]{0,1:T(1,128)} %copy-done.8) | copy-start | bytes 12292
  442.6 69.6 %all-to-all-start.4 = ((bf16[128,16,1280]{2,1,0:T(8,128)(2,1)}), bf16[128,16,1280]{2,1,0:T(8,128)(2,1)}, u32[]{:S(2)}, u32[]{:S(2)}) async-start(bf16[128,16,1280]{2,1,0:T(8,128)(2,1)} %reshape.238), calls=%async_computation.4 | async-start | bytes 10485760 | tf_op jit(solution)/shard_map/all_to_all | solution.py:61
  460.8 4.0 copy-start
  522.1 4.0 copy-start.1

commit v3 on v2

--- a/solution.py
+++ b/solution.py
@@ -5,6 +5,7 @@
 
 STRATA = 8
 LEVELS = 64
+CHUNK_SIZES = (5, 5)
 
 
 def expert_grads(inputs, upstream, weight_in, weight_out):
@@ -52,37 +53,46 @@
     padded_upstream = jnp.concatenate([upstream, jnp.zeros((1, width), jnp.bfloat16)], axis=0)
     weight_in = w_gate_up[0]
     weight_out = w_down[0]
-    chunks = 2 if capacity % 2 == 0 else 1
-    per_chunk = capacity // chunks
-    block_rows = 16 if (per_chunk * width) % (16 * 128) == 0 else per_chunk
-    block = (device_count, block_rows, per_chunk * width // block_rows)
-    chunk_slots = device_count * per_chunk
+    sizes = CHUNK_SIZES if sum(CHUNK_SIZES) == capacity else (capacity,)
+    starts = [sum(sizes[:c]) for c in range(len(sizes))]
+    tiled = all((n * width) % (16 * 128) == 0 for n in sizes)
+    rows = 16 if tiled else 1
+
+    def block_of(n):
+        return (device_count, rows, n * width // rows)
+
     def exchange(part):
         return lax.all_to_all(part, axes, 0, 0, tiled=True)
 
     def send_of(c):
-        index = token_index[:, c * per_chunk : (c + 1) * per_chunk].reshape(-1)
+        index = token_index[:, starts[c] : starts[c] + sizes[c]].reshape(-1)
         return jnp.concatenate(
-            [padded_tokens[index].reshape(block), padded_upstream[index].reshape(block)], axis=1
+            [
+                padded_tokens[index].reshape(block_of(sizes[c])),
+                padded_upstream[index].reshape(block_of(sizes[c])),
+            ],
+            axis=1,
         )
 
-    def compute(arrived):
+    def compute(c, arrived):
+        n = sizes[c]
         row_grads, prob_grad = expert_grads(
-            arrived[:, :block_rows].reshape(chunk_slots, width),
-            arrived[:, block_rows:].reshape(chunk_slots, width),
+            arrived[:, :rows].reshape(device_count * n, width),
+            arrived[:, rows:].reshape(device_count * n, width),
             weight_in,
             weight_out,
         )
-        return row_grads.reshape(block), prob_grad.reshape(device_count, 1, per_chunk)
+        return row_grads.reshape(block_of(n)), prob_grad.reshape(device_count, n)
 
     def combine(c, home):
-        local = ranking - c * per_chunk
-        inside = (local >= 0) & (local < per_chunk)
-        slot = jnp.where(inside, chosen * per_chunk + local, -1).reshape(token_rows, chosen_count)
+        n = sizes[c]
+        local = ranking - starts[c]
+        inside = (local >= 0) & (local < n)
+        slot = jnp.where(inside, chosen * n + local, -1).reshape(token_rows, chosen_count)
         weight = jnp.where(inside.reshape(token_rows, chosen_count), gate_probs, 0.0)
         table = jnp.sum(
             jnp.where(
-                slot[:, :, None] == jnp.arange(chunk_slots, dtype=jnp.int32)[None, None, :],
+                slot[:, :, None] == jnp.arange(device_count * n, dtype=jnp.int32)[None, None, :],
                 weight[:, :, None],
                 0.0,
             ),
@@ -90,34 +100,45 @@
         )
         high = table.astype(jnp.bfloat16)
         low = (table - high.astype(jnp.float32)).astype(jnp.bfloat16)
-        home = home.reshape(chunk_slots, width)
+        home = home.reshape(device_count * n, width)
         return jnp.dot(high, home, preferred_element_type=jnp.float32) + jnp.dot(
             low, home, preferred_element_type=jnp.float32
         )
+
+    last = len(sizes) - 1
+    extra = rows * 128 if rows * 128 >= capacity else capacity
+    extra_cols = extra // rows
 
     arrived = exchange(send_of(0))
     grad_tokens = None
     prob_parts = []
     pending = None
-    for c in range(chunks):
-        row_grads, prob_grad = compute(arrived)
-        if c + 1 < chunks:
+    for c in range(len(sizes)):
+        row_grads, prob_grad = compute(c, arrived)
+        prob_parts.append(prob_grad)
+        if c < last:
             arrived = exchange(send_of(c + 1))
-            arrived, row_grads, prob_grad = lax.optimization_barrier(
-                (arrived, row_grads, prob_grad)
+            arrived, row_grads, prob_parts = lax.optimization_barrier(
+                (arrived, row_grads, prob_parts)
             )
         if pending is not None:
-            pending, row_grads, prob_grad = lax.optimization_barrier(
-                (pending, row_grads, prob_grad)
+            pending, row_grads, prob_parts = lax.optimization_barrier(
+                (pending, row_grads, prob_parts)
             )
-            part = combine(c - 1, pending[0])
-            prob_parts.append(pending[1].reshape(device_count, per_chunk))
+            part = combine(c - 1, pending)
             grad_tokens = part if grad_tokens is None else grad_tokens + part
-        pending = (exchange(row_grads), exchange(prob_grad))
-    part = combine(chunks - 1, pending[0])
-    prob_parts.append(pending[1].reshape(device_count, per_chunk))
+        if c < last:
+            pending = exchange(row_grads)
+        else:
+            probs = jnp.concatenate(prob_parts, axis=1)
+            probs = jnp.pad(probs, ((0, 0), (0, extra - capacity))).reshape(
+                device_count, rows, extra_cols
+            )
+            pending = exchange(jnp.concatenate([row_grads, probs], axis=2))
+    row_cols = sizes[last] * width // rows
+    part = combine(last, pending[:, :, :row_cols])
     grad_tokens = part if grad_tokens is None else grad_tokens + part
-    home_probs = jnp.concatenate(prob_parts, axis=1).reshape(-1)
+    home_probs = pending[:, :, row_cols:].reshape(device_count, extra)[:, :capacity].reshape(-1)
     grad_probs = home_probs[placed].reshape(token_rows, chosen_count)
     return (grad_tokens.astype(jnp.bfloat16), grad_probs)
 

time: 537 us -> 533 us (level)
  blocking collectives: 36 us -> 0 us
  waiting for transfers between devices: 197 us -> 211 us
  starting transfers between devices: 32.5 us -> 39.3 us
  local copies, waits for them, and re-layouts: 175 us -> 181 us
  other arithmetic: 26.4 us -> 31.8 us
    all_to_all x2 -> x0, blocking collectives: 36 us -> none  [exchange(): return lax.all_to_all(part, axes, 0, 0, tiled=True)]
    all_to_all x4, waiting for transfers between devices: 197 us -> 211 us  [exchange(): return lax.all_to_all(part, axes, 0, 0, tiled=True)]
    all_to_all x4, starting transfers between devices: 32.5 us -> 39.3 us  [exchange(): return lax.all_to_all(part, axes, 0, 0, tiled=True)]
    slice x3 -> x6, local copies, waits for them, and re-layouts: 17.4 us -> 23.7 us  [the longest x2 17.4 us: compute(): arrived[:, :rows].reshape(device_count * n, width)]
    concatenate x3 -> x4, other arithmetic: 20.5 us -> 25.9 us  [the longest x2 20.4 us: send_of(): jnp.concatenate([padded_tokens[index].reshape(block_of(sizes[c])), padded...]
    reshape x15 -> x16, local copies, waits for them, and re-layouts: 120 us -> 120 us  [the longest x2 20 us: compute(): arrived[:, :rows].reshape(device_count * n, width)]
  transfers between devices with their start and end apart: 4 -> 4, of which waited for: 4 -> 3; matrix products, arithmetic and copies ran while one was open for 36% -> 35% of each run, Pallas kernels for 0% -> 0%
where the time goes in v3:
time: 533 us; the launch traced here: 525 us
  waiting for transfers between devices  211 us (40%)
  local copies, waits for them, and re-layouts  181 us (34%)
  matrix products  60 us (11%)
  starting transfers between devices  39.3 us (7%)
  other arithmetic  31.8 us (6%)
    all_to_all x4, waiting for transfers between devices, exchange(): return lax.all_to_all(part, axes, 0, 0, tiled=True)  211 us
    all_to_all x4, starting transfers between devices, exchange(): return lax.all_to_all(part, axes, 0, 0, tiled=True)  39.3 us
    dot_general x2, matrix products, expert_grads(): projected = jnp.dot(inputs, weight_in, preferred_element_type=jnp.float32)  21.9 us
    concatenate x2, other arithmetic, send_of(): jnp.concatenate([padded_tokens[index].reshape(block_of(sizes[c])), padded...  20.4 us
    reshape x2, local copies, waits for them, and re-layouts, compute(): arrived[:, :rows].reshape(device_count * n, width)  20 us
    reshape x2, local copies, waits for them, and re-layouts, send_of(): padded_upstream[index].reshape(block_of(sizes[c]))  19.9 us
    reshape x2, local copies, waits for them, and re-layouts, combine(): home = home.reshape(device_count * n, width)  19.9 us
    reshape x2, local copies, waits for them, and re-layouts, compute(): return (row_grads.reshape(block_of(n)), prob_grad.reshape(device_count, n))  19.9 us
  transfers between devices with their start and end apart: 4, of which 3 were waited for; matrix products, arithmetic and copies ran while one was open for 35% of the time, Pallas kernels for 0%

profile of v3, /device:TPU:1, one launch (start us, length us, event | category | flops | bytes accessed | tf_op | source)
XLA Modules:
  0.0 524.8 jit_solution(14598598143832050393)
XLA Ops:
  17.7 10.0 %reshape.214 = bf16[128,16,1280]{2,1,0:T(8,128)(2,1)} reshape(bf16[640,4096]{1,0:T(8,128)(2,1)} %gather_fusion.3) | data formatting | bytes 10485760 | tf_op jit(solution)/shard_map/reshape | solution.py:72
  33.2 9.9 %reshape.213 = bf16[128,16,1280]{2,1,0:T(8,128)(2,1)} reshape(bf16[640,4096]{1,0:T(8,128)(2,1)} %gather_fusion.2) | data formatting | bytes 10485760 | tf_op jit(solution)/shard_map/reshape | solution.py:71
  43.1 10.2 %pad_maximum_fusion.1 = bf16[128,32,1280]{2,1,0:T(8,128)(2,1)} fusion(bf16[128,16,1280]{2,1,0:T(8,128)(2,1)} %reshape.214, bf16[128,16,1280]{2,1,0:T(8,128)(2,1)} %reshape.213), kind=kLoop, calls=%fused_computation.7 | loop fusion | flops 20971520 | bytes 20971520 | tf_op jit(solution)/shard_map/concatenate | solution.py:69
  53.3 12.4 %all-to-all-start.1 = ((bf16[128,32,1280]{2,1,0:T(8,128)(2,1)}), bf16[128,32,1280]{2,1,0:T(8,128)(2,1)}, u32[]{:S(2)}, u32[]{:S(2)}) async-start(bf16[128,32,1280]{2,1,0:T(8,128)(2,1)} %pad_maximum_fusion.1), calls=%async_computation.1 | async-start | bytes 20971520 | tf_op jit(solution)/shard_map/all_to_all | solution.py:65
  76.5 9.9 %reshape.211 = bf16[128,16,1280]{2,1,0:T(8,128)(2,1)} reshape(bf16[640,4096]{1,0:T(8,128)(2,1)} %gather_fusion.1) | data formatting | bytes 10485760 | tf_op jit(solution)/shard_map/reshape | solution.py:72
  86.4 9.9 %reshape.210 = bf16[128,16,1280]{2,1,0:T(8,128)(2,1)} reshape(bf16[640,4096]{1,0:T(8,128)(2,1)} %gather_fusion) | data formatting | bytes 10485760 | tf_op jit(solution)/shard_map/reshape | solution.py:71
  96.3 10.2 %pad_maximum_fusion = bf16[128,32,1280]{2,1,0:T(8,128)(2,1)} fusion(bf16[128,16,1280]{2,1,0:T(8,128)(2,1)} %reshape.211, bf16[128,16,1280]{2,1,0:T(8,128)(2,1)} %reshape.210), kind=kLoop, calls=%fused_computation.6 | loop fusion | flops 20971520 | bytes 20971520 | tf_op jit(solution)/shard_map/concatenate | solution.py:69
  106.5 90.7 %all-to-all-done.1 = bf16[128,32,1280]{2,1,0:T(8,128)(2,1)} async-done(((bf16[128,32,1280]{2,1,0:T(8,128)(2,1)}), bf16[128,32,1280]{2,1,0:T(8,128)(2,1)}, u32[]{:S(2)}, u32[]{:S(2)}) %all-to-all-start.1) | async-done | bytes 10485792 | tf_op jit(solution)/shard_map/all_to_all | solution.py:65
  214.4 10.0 %reshape.216 = bf16[640,4096]{1,0:T(8,128)(2,1)} reshape(bf16[128,16,1280]{2,1,0:T(8,128)(2,1)} %get-tuple-element.24) | data formatting | bytes 10485760 | tf_op jit(solution)/shard_map/reshape | solution.py:80
  224.4 9.9 %reshape.215 = bf16[640,4096]{1,0:T(8,128)(2,1)} reshape(bf16[128,16,1280]{2,1,0:T(8,128)(2,1)} %get-tuple-element.25) | data formatting | bytes 10485760 | tf_op jit(solution)/shard_map/reshape | solution.py:81
  234.3 10.9 %fusion.6 = f32[640,1024]{0,1:T(8,128)S(1)} fusion(bf16[640,4096]{1,0:T(8,128)(2,1)} %reshape.216, bf16[1,4096,1024]{2,1,0:T(8,128)(2,1)} %param.14), kind=kOutput, calls=%fused_computation.14 | convolution fusion | flops 5368709120 | bytes 16252928 | tf_op jit(solution)/shard_map/dot_general | solution.py:13
  249.2 9.9 %fusion.8 = bf16[640,4096]{1,0:T(8,128)(2,1)} fusion(bf16[1,4096,1024]{2,1,0:T(8,128)(2,1)} %param.14, bf16[640,512]{0,1:T(8,128)(2,1)S(1)} %get-tuple-element.30, bf16[640,512]{0,1:T(8,128)(2,1)S(1)} %get-tuple-element.31), kind=kOutput, calls=%fused_computation.16 | convolution fusion | flops 5373952000 | bytes 14942208 | tf_op jit(solution)/shard_map/dot_general | solution.py:24
  259.1 10.0 %reshape.217 = bf16[128,16,1280]{2,1,0:T(8,128)(2,1)} reshape(bf16[640,4096]{1,0:T(8,128)(2,1)} %fusion.8) | data formatting | bytes 10485760 | tf_op jit(solution)/shard_map/reshape | solution.py:85
  269.3 68.0 %all-to-all-done = bf16[128,32,1280]{2,1,0:T(8,128)(2,1)} async-done(((bf16[128,32,1280]{2,1,0:T(8,128)(2,1)}), bf16[128,32,1280]{2,1,0:T(8,128)(2,1)}, u32[]{:S(2)}, u32[]{:S(2)}) %all-to-all-start) | async-done | bytes 10485792 | tf_op jit(solution)/shard_map/all_to_all | solution.py:65
  345.1 8.7 %fusion.51 = (bf16[128,16,1280]{2,1,0:T(8,128)(2,1)}, bf16[128,16,1280]{2,1,0:T(8,128)(2,1)}) fusion(bf16[128,32,1280]{2,1,0:T(8,128)(2,1)} %all-to-all-done), kind=kLoop, calls=%fused_computation.100 | loop fusion | bytes 20971520 | tf_op jit(solution)/shard_map/slice | solution.py:80
  353.9 9.9 %reshape.219 = bf16[640,4096]{1,0:T(8,128)(2,1)} reshape(bf16[128,16,1280]{2,1,0:T(8,128)(2,1)} %get-tuple-element.22) | data formatting | bytes 10485760 | tf_op jit(solution)/shard_map/reshape | solution.py:80
  363.8 9.9 %reshape.218 = bf16[640,4096]{1,0:T(8,128)(2,1)} reshape(bf16[128,16,1280]{2,1,0:T(8,128)(2,1)} %get-tuple-element.23) | data formatting | bytes 10485760 | tf_op jit(solution)/shard_map/reshape | solution.py:81
  373.7 10.9 %fusion.2 = f32[640,1024]{0,1:T(8,128)S(1)} fusion(bf16[640,4096]{1,0:T(8,128)(2,1)} %reshape.219, bf16[1,4096,1024]{2,1,0:T(8,128)(2,1)} %param.14), kind=kOutput, calls=%fused_computation.10 | convolution fusion | flops 5368709120 | bytes 16252928 | tf_op jit(solution)/shard_map/dot_general | solution.py:13
  388.6 9.9 %fusion.11 = bf16[640,4096]{1,0:T(8,128)(2,1)} fusion(bf16[1,4096,1024]{2,1,0:T(8,128)(2,1)} %param.14, bf16[640,512]{0,1:T(8,128)(2,1)S(1)} %get-tuple-element.27, bf16[640,512]{0,1:T(8,128)(2,1)S(1)} %get-tuple-element.28), kind=kOutput, calls=%fused_computation.17 | convolution fusion | flops 5373952000 | bytes 14942208 | tf_op jit(solution)/shard_map/dot_general | solution.py:24
  398.6 9.9 %reshape.220 = bf16[128,16,1280]{2,1,0:T(8,128)(2,1)} reshape(bf16[640,4096]{1,0:T(8,128)(2,1)} %fusion.11) | data formatting | bytes 10485760 | tf_op jit(solution)/shard_map/reshape | solution.py:85
  414.8 10.6 %all-to-all-start.3 = ((bf16[128,16,1408]{2,1,0:T(8,128)(2,1)}), bf16[128,16,1408]{2,1,0:T(8,128)(2,1)}, u32[]{:S(2)}, u32[]{:S(2)}) async-start(bf16[128,16,1408]{2,1,0:T(8,128)(2,1)} %pad_maximum_fusion.2), calls=%async_computation.3 | async-start | bytes 11534336 | tf_op jit(solution)/shard_map/all_to_all | solution.py:65
  427.6 9.9 %reshape.221 = bf16[640,4096]{1,0:T(8,128)(2,1)} reshape(bf16[128,16,1280]{2,1,0:T(8,128)(2,1)} %all-to-all-done.2) | data formatting | bytes 10485760 | tf_op jit(solution)/shard_map/reshape | solution.py:103
  442.6 52.0 %all-to-all-done.3 = bf16[128,16,1408]{2,1,0:T(8,128)(2,1)} async-done(((bf16[128,16,1408]{2,1,0:T(8,128)(2,1)}), bf16[128,16,1408]{2,1,0:T(8,128)(2,1)}, u32[]{:S(2)}, u32[]{:S(2)}) %all-to-all-start.3) | async-done | bytes 5767200 | tf_op jit(solution)/shard_map/all_to_all | solution.py:65
  499.8 9.9 %reshape.223 = bf16[640,4096]{1,0:T(8,128)(2,1)} reshape(bf16[128,16,1280]{2,1,0:T(8,128)(2,1)} %slice.80) | data formatting | bytes 10485760 | tf_op jit(solution)/shard_map/reshape | solution.py:103
  (95 shorter events, 99.1 us)
Async XLA Ops:
  4.0 0.6 copy-start.4
  4.6 4.3 copy-start.7
  17.7 10.0 %copy-start.3 = (bf16[128,4096]{1,0:T(8,128)(2,1)S(1)}, bf16[128,4096]{1,0:T(8,128)(2,1)}, u32[]{:S(2)}) copy-start(bf16[128,4096]{1,0:T(8,128)(2,1)} %param.8) | copy-start | bytes 3145732
  53.3 143.9 %all-to-all-start.1 = ((bf16[128,32,1280]{2,1,0:T(8,128)(2,1)}), bf16[128,32,1280]{2,1,0:T(8,128)(2,1)}, u32[]{:S(2)}, u32[]{:S(2)}) async-start(bf16[128,32,1280]{2,1,0:T(8,128)(2,1)} %pad_maximum_fusion.1), calls=%async_computation.1 | async-start | bytes 20971520 | tf_op jit(solution)/shard_map/all_to_all | solution.py:65
  197.2 140.1 %all-to-all-start = ((bf16[128,32,1280]{2,1,0:T(8,128)(2,1)}), bf16[128,32,1280]{2,1,0:T(8,128)(2,1)}, u32[]{:S(2)}, u32[]{:S(2)}) async-start(bf16[128,32,1280]{2,1,0:T(8,128)(2,1)} %pad_maximum_fusion), calls=%async_computation | async-start | bytes 20971520 | tf_op jit(solution)/shard_map/all_to_all | solution.py:65
  234.3 11.0 %copy-start.1 = (bf16[640,4096]{1,0:T(8,128)(2,1)S(1)}, bf16[640,4096]{1,0:T(8,128)(2,1)}, u32[]{:S(2)}) copy-start(bf16[640,4096]{1,0:T(8,128)(2,1)} %reshape.215) | copy-start | bytes 15728644
  234.3 11.0 %copy-start.10 = (bf16[1,512,4096]{2,1,0:T(8,128)(2,1)S(1)}, bf16[1,512,4096]{2,1,0:T(8,128)(2,1)}, u32[]{:S(2)}) copy-start(bf16[1,512,4096]{2,1,0:T(8,128)(2,1)} %param.15) | copy-start | bytes 12582916
  337.3 71.4 %all-to-all-start.2 = ((bf16[128,16,1280]{2,1,0:T(8,128)(2,1)}), bf16[128,16,1280]{2,1,0:T(8,128)(2,1)}, u32[]{:S(2)}, u32[]{:S(2)}) async-start(bf16[128,16,1280]{2,1,0:T(8,128)(2,1)} %reshape.217), calls=%async_computation.2 | async-start | bytes 10485760 | tf_op jit(solution)/shard_map/all_to_all | solution.py:65
  373.7 11.0 %copy-start.2 = (bf16[640,4096]{1,0:T(8,128)(2,1)S(1)}, bf16[640,4096]{1,0:T(8,128)(2,1)}, u32[]{:S(2)}) copy-start(bf16[640,4096]{1,0:T(8,128)(2,1)} %reshape.218) | copy-start | bytes 15728644
  373.7 11.0 %copy-start.11 = (bf16[1,512,4096]{2,1,0:T(8,128)(2,1)S(1)}, bf16[1,512,4096]{2,1,0:T(8,128)(2,1)}, u32[]{:S(2)}) copy-start(bf16[1,512,4096]{2,1,0:T(8,128)(2,1)} %param.15) | copy-start | bytes 12582916
  414.8 10.6 %copy-start.5 = (s32[1024]{0:T(1024)S(1)}, s32[1024]{0:T(1024)}, u32[]{:S(2)}) copy-start(s32[1024]{0:T(1024)} %copy-done.4) | copy-start | bytes 12292
  414.8 10.7 %copy-start.6 = (s32[128,8]{0,1:T(8,128)S(1)}, s32[128,8]{0,1:T(8,128)}, u32[]{:S(2)}) copy-start(s32[128,8]{0,1:T(8,128)} %get-tuple-element.38) | copy-start | bytes 12292
  414.8 10.8 %copy-start.9 = (f32[128,8]{0,1:T(8,128)S(1)}, f32[128,8]{0,1:T(8,128)}, u32[]{:S(2)}) copy-start(f32[128,8]{0,1:T(8,128)} %param.10) | copy-start | bytes 12292
  414.8 10.9 %copy-start.8 = (s32[1024,1]{0,1:T(1,128)S(1)}, s32[1024,1]{0,1:T(1,128)}, u32[]{:S(2)}) copy-start(s32[1024,1]{0,1:T(1,128)} %copy-done.7) | copy-start | bytes 12292
  414.8 79.8 %all-to-all-start.3 = ((bf16[128,16,1408]{2,1,0:T(8,128)(2,1)}), bf16[128,16,1408]{2,1,0:T(8,128)(2,1)}, u32[]{:S(2)}, u32[]{:S(2)}) async-start(bf16[128,16,1408]{2,1,0:T(8,128)(2,1)} %pad_maximum_fusion.2), calls=%async_computation.3 | async-start | bytes 11534336 | tf_op jit(solution)/shard_map/all_to_all | solution.py:65
  437.5 4.0 copy-start
  511.1 11.2 %slice-start = ((s8[5242880]{0:T(1024)(128)(4,1)}), s8[1048576]{0:T(1024)(128)(4,1)S(1)}, s32[]{:S(2)}) async-start(s8[5242880]{0:T(1024)(128)(4,1)} %bitcast.47), calls=%async_computation.4 | async-start | bytes 2097152
  518.7 3.7 slice-start.1
